TPU v7x, 32 devices: a whole 2x2x4 slice. The times are simulated.
32 devices in a mesh: illum: 8 (over z, y), tile: 4 (over x, core).
Axes of the slice: x: 2, y: 2, z: 4, core: 2. Of those that a mesh axis runs over, the one named last changes fastest.
Arguments:
- tilts: int32 [8, 2], P('illum'), may hold values from -64 to 64
- taps: float32 [2, 33], replicated, may hold values from -0.75 to 0.75
- stored_planes: float32 [2, 128, 4096], P(None, 'tile', 'illum'), may hold values from -3.140625 to 3.140625
- owner: int32 [2, 8], replicated, may hold values from 0 to 7, each once within a row
Outputs:
- exit_field: float32 [2, 8, 128, 4096], P(None, 'illum', 'tile')
Inputs may be any that keep to these rules, and one draw needn't show every extreme that they name: Each row of owner is a permutation of the 8 stored column blocks.
All inputs are finite; a program needn't handle non-finite values.
Results may differ from a plain program's by a relative error of at most 0.0003.
Values sent between devices are 32-bit elements; how exact they have to be, the bound alone decides.
No kernel may reach another device: no remote copies, remote signals or barrier semaphores. Data moves between devices by JAX's collectives and lax.ppermute only.
A program may use at most 64 MiB of HBM per device.

v0:
```python
import jax
import jax.numpy as jnp
from jax import lax
from jax.sharding import PartitionSpec as P

NY = 4096
PLANES = 2
HALF = 16
two_pi = 6.283185307179586


def extended(cells, sides, width):
    for axis, dim in sides:
        count = lax.axis_size(axis)
        ends = count - 1
        head = lax.slice_in_dim(cells, 0, width, axis=dim)
        tail = lax.slice_in_dim(cells, cells.shape[dim] - width, cells.shape[dim], axis=dim)
        cells = jnp.concatenate(
            [
                lax.ppermute(tail, axis, [(i, (i + 1) % count) for i in range(ends)]),
                cells,
                lax.ppermute(head, axis, [((i + 1) % count, i) for i in range(ends)]),
            ],
            axis=dim,
        )
    return cells


def toeplitz(tap_row, block):
    rows = jnp.arange(block + 2 * HALF)[:, None]
    cols = jnp.arange(block)[None, :]
    offset = rows - cols
    steps = jnp.arange(2 * HALF + 1)
    return jnp.sum(jnp.where(offset[:, :, None] == steps, tap_row, 0.0), axis=2)


def band_matrix(tap_row, count):
    rows = jnp.arange(count)[:, None]
    cols = jnp.arange(count + 2 * HALF)[None, :]
    offset = cols - rows
    steps = jnp.arange(2 * HALF + 1)
    return jnp.sum(jnp.where(offset[:, :, None] == steps, tap_row, 0.0), axis=2)


def windows(field, block):
    length = field.shape[-1]
    count = length // block
    widths = [(0, 0)] * (field.ndim - 1) + [(HALF, block - HALF)]
    padded = jnp.pad(field, widths)
    lead = field.shape[:-1]
    main = padded[..., :length].reshape(lead + (count, block))
    after = padded[..., block : length + block].reshape(lead + (count, block))[..., : 2 * HALF]
    return jnp.concatenate([main, after], axis=-1)


def along_pass(real, imag, taps):
    block = min(128, real.shape[-1])
    win_real = windows(real, block)
    win_imag = windows(imag, block)
    kern_real = toeplitz(taps[0], block)
    kern_imag = toeplitz(taps[1], block)

    def apply(win, kern):
        out = jnp.einsum("...nj,jc->...nc", win, kern, precision=lax.Precision.HIGHEST)
        return out.reshape(real.shape)

    return (
        apply(win_real, kern_real) - apply(win_imag, kern_imag),
        apply(win_real, kern_imag) + apply(win_imag, kern_real),
    )


def cross_pass(real, imag, taps):
    count = real.shape[1] - 2 * HALF
    band_real = band_matrix(taps[0], count)
    band_imag = band_matrix(taps[1], count)

    def apply(band, field):
        return jnp.einsum("ij,ajy->aiy", band, field, precision=lax.Precision.HIGHEST)

    return (
        apply(band_real, real) - apply(band_imag, imag),
        apply(band_real, imag) + apply(band_imag, real),
    )


def transmit(real, imag, screen):
    cosine = jnp.cos(screen)
    sine = jnp.sin(screen)
    return (real * cosine - imag * sine, real * sine + imag * cosine)


def reorder(gathered, owner):
    count = gathered.shape[1]
    blocks = owner.shape[1]
    width = gathered.shape[2] // blocks
    planes = [
        gathered[p].reshape(count, blocks, width)[:, owner[p], :].reshape(count, blocks * width)
        for p in range(gathered.shape[0])
    ]
    return jnp.stack(planes)


def body(tilts, taps, stored_planes, owner):
    local_rows = stored_planes.shape[1]
    total_rows = local_rows * lax.axis_size("tile")
    total_cols = NY
    first_row = lax.axis_index("tile") * local_rows
    gathered = lax.all_gather(stored_planes, "illum", axis=2, tiled=True)
    screens = reorder(gathered, owner)
    extra = 0
    span = local_rows + 2 * extra
    global_rows = first_row - extra + jnp.arange(span, dtype=jnp.int32)
    inside = (global_rows >= 0) & (global_rows < total_rows)
    cols = jnp.arange(total_cols, dtype=jnp.int32)
    across = (
        jnp.mod(tilts[:, 0:1] * global_rows[None, :], total_rows).astype(jnp.float32) / total_rows
    )
    along = jnp.mod(tilts[:, 1:2] * cols[None, :], total_cols).astype(jnp.float32) / total_cols
    theta = two_pi * (across[:, :, None] + along[:, None, :])
    real = jnp.where(inside[None, :, None], jnp.cos(theta), 0.0)
    imag = jnp.where(inside[None, :, None], jnp.sin(theta), 0.0)
    for plane in range(PLANES):
        real, imag = transmit(real, imag, screens[plane])
        packed = extended(jnp.stack([real, imag]), (("tile", 2),), HALF)
        real, imag = cross_pass(packed[0], packed[1], taps)
        real, imag = along_pass(real, imag, taps)
    return jnp.stack([real, imag])


def solution(mesh):
    in_specs = (P("illum", None), P(), P(None, "tile", "illum"), P())
    out_specs = P(None, "illum", "tile", None)
    return jax.shard_map(body, mesh=mesh, in_specs=in_specs, out_specs=out_specs, check_vma=False)
```

profile of v0, /device:TPU:1, one launch (start us, length us, event | category | flops | bytes accessed | tf_op | source)
XLA Modules:
  0.0 116.0 jit_solution(4339684245039347680)
XLA Ops:
  6.5 0.7 all-gather.2.cloned.1.call-update
  7.3 1.4 %fusion.42 = (s32[1,1]{1,0:T(1,128)}, s32[1,1]{1,0:T(1,128)}) fusion(s32[1,2]{1,0:T(1,128)} %param.4), kind=kLoop, calls=%fused_computation.110 | loop fusion | bytes 16 | tf_op jit(solution)/shard_map/slice | solution.py:117
  9.3 0.8 fusion.32
  10.1 0.7 fusion.24
  10.8 0.8 slice_bitcast_fusion.20
  11.8 39.1 %all-gather.2.cloned.1.call-done = f32[2,32,4096]{2,1,0:T(8,128)} async-done(((f32[2,32,512]{2,1,0:T(8,128)}), f32[2,32,4096]{2,1,0:T(8,128)}) %all-gather.2.cloned.1.call-update) | async-done | bytes 1048592 | tf_op jit(solution)/shard_map/all_gather | solution.py:109
  50.9 1.3 %fusion.41 = (f32[1,32,4096]{2,1,0:T(8,128)S(1)}, f32[1,32,4096]{2,1,0:T(8,128)S(1)}) fusion(f32[2,32,4096]{2,1,0:T(8,128)} %all-gather.2.cloned.1.call-done), kind=kLoop, calls=%fused_computation.109 | loop fusion | bytes 2097152 | tf_op jit(solution)/shard_map/slice | solution.py:98
  53.4 1.9 %sine_bitcast_fusion.1 = (f32[32,8,512]{2,0,1:T(8,128)S(1)}, f32[32,8,512]{2,0,1:T(8,128)S(1)}) fusion(f32[8,32,512]{2,1,0:T(8,128)S(1)} %gather_fusion), kind=kLoop, calls=%fused_computation.49 | loop fusion | bytes 1572864 | tf_op jit(solution)/shard_map/sin | solution.py:89
  56.1 2.2 %multiply_subtract_fusion.1 = (f32[1,1,32,4096]{3,2,1,0:T(8,128)S(1)}, f32[1,1,32,4096]{3,2,1,0:T(8,128)S(1)}) fusion(f32[1,1,32,4096]{3,2,1,0:T(8,128)S(1)} %sin.57, f32[1,1,32,4096]{3,2,1,0:T(8,128)S(1)} %cos.57, f32[4096]{0:T(1024)S(1)} %fusion.24, f32[32]{0:T(128)S(1)} %fusion.29, pred[32]{0:T(512)(128)(4,1)S(1)} %compare_and_fusion), kind=kLoop, calls=%fused_computation.62 | loop fusion | flops 1310720 | bytes 2113696 | tf_op jit(solution)/shard_map/sub | solution.py:90
  58.2 0.9 fusion.13
  59.1 4.6 %collective-permute-start = (f32[2,1,16,4096]{3,2,1,0:T(8,128)}, f32[2,1,16,4096]{3,2,1,0:T(8,128)}, u32[]{:S(2)}, u32[]{:S(2)}) collective-permute-start(f32[2,1,16,4096]{3,2,1,0:T(8,128)} %get-tuple-element.17), channel_id=1, source_target_pairs={{0,1},{1,2},{2,3},{4,5},{5,6},{6,7},{8,9},{9,10},{10,11},{12,13},{... | collective-permute-start | bytes 1572872 | tf_op jit(solution)/shard_map/ppermute | solution.py:20
  63.8 2.1 %collective-permute-start.1 = (f32[2,1,16,4096]{3,2,1,0:T(8,128)S(1)}, f32[2,1,16,4096]{3,2,1,0:T(8,128)}, u32[]{:S(2)}, u32[]{:S(2)}) collective-permute-start(f32[2,1,16,4096]{3,2,1,0:T(8,128)S(1)} %get-tuple-element.18), channel_id=1, source_target_pairs={{1,0},{2,1},{3,2},{5,4},{6,5},{7,6},{9,8},{10,9},{11,10},{13,12},{... | collective-permute-start | bytes 1572872 | tf_op jit(solution)/shard_map/ppermute | solution.py:22
  67.7 1.9 %sine_bitcast_fusion = (f32[32,8,512]{2,0,1:T(8,128)S(1)}, f32[32,8,512]{2,0,1:T(8,128)S(1)}) fusion(f32[8,32,512]{2,1,0:T(8,128)S(1)} %gather_fusion.1), kind=kLoop, calls=%fused_computation.47 | loop fusion | bytes 1572864 | tf_op jit(solution)/shard_map/sin | solution.py:89
  70.4 4.0 %collective-permute-done.1 = f32[2,1,16,4096]{3,2,1,0:T(8,128)} collective-permute-done((f32[2,1,16,4096]{3,2,1,0:T(8,128)S(1)}, f32[2,1,16,4096]{3,2,1,0:T(8,128)}, u32[]{:S(2)}, u32[]{:S(2)}) %collective-permute-start.1) | collective-permute-done | bytes 524320 | tf_op jit(solution)/shard_map/ppermute | solution.py:22
  74.4 1.3 %pad_maximum_fusion = f32[2,1,64,4096]{3,2,1,0:T(8,128)S(1)} fusion(f32[2,1,16,4096]{3,2,1,0:T(8,128)} %collective-permute-done.1, f32[1,1,32,4096]{3,2,1,0:T(8,128)S(1)} %get-tuple-element.12, f32[1,1,32,4096]{3,2,1,0:T(8,128)S(1)} %get-tuple-element.11, f32[2,1,16,4096]{3,2,1,0:T(8,128)} %collective-permute-done), kind=kLoop, calls=%fused_computation.13 | loop fusion | flops 1572864 | bytes 4194304 | tf_op jit(solution)/shard_map/concatenate | solution.py:18
  77.1 0.7 fusion
  78.3 0.7 fusion.1
  79.6 1.0 fusion.11
  80.5 1.0 fusion.10
  81.5 1.8 %convolution_subtract_fusion.3 = f32[32,32,128]{2,1,0:T(8,128)} fusion(f32[32,32,128]{2,1,0:T(8,128)S(1)} %fusion.11, f32[1,32,32,32]{3,2,1,0:T(8,128)S(1)} %bitcast.154, f32[1,32,32,128]{3,2,1,0:T(8,128)S(1)} %bitcast.156, f32[160,128]{1,0:T(8,128)S(1)} %get-tuple-element.6), kind=kOutput, calls=%fused_computation.18 | convolution fusion | flops 251953152 | bytes 1785856 | tf_op jit(solution)/shard_map/...nj,jc->...nc/dot_general | solution.py:64
  83.3 1.1 sub.176
  84.4 1.8 %convolution_add_fusion.3 = f32[32,32,128]{2,1,0:T(8,128)} fusion(f32[32,32,128]{2,1,0:T(8,128)S(1)} %fusion.10, f32[1,32,32,32]{3,2,1,0:T(8,128)S(1)} %bitcast.155, f32[1,32,32,128]{3,2,1,0:T(8,128)S(1)} %bitcast.157, f32[160,128]{1,0:T(8,128)S(1)} %get-tuple-element.5), kind=kOutput, calls=%fused_computation.17 | convolution fusion | flops 251953152 | bytes 1785856 | tf_op jit(solution)/shard_map/...nj,jc->...nc/dot_general | solution.py:64
  86.2 1.1 add.184
  87.5 1.9 %collective-permute-start.2 = (f32[2,1,16,4096]{3,2,1,0:T(8,128)S(1)}, f32[2,1,16,4096]{3,2,1,0:T(8,128)S(1)}, u32[]{:S(2)}, u32[]{:S(2)}) collective-permute-start(f32[2,1,16,4096]{3,2,1,0:T(8,128)S(1)} %get-tuple-element.13), channel_id=1, source_target_pairs={{0,1},{1,2},{2,3},{4,5},{5,6},{6,7},{8,9},{9,10},{10,11},{12,13},{... | collective-permute-start | bytes 1572872 | tf_op jit(solution)/shard_map/ppermute | solution.py:20
  89.5 2.7 %collective-permute-start.3 = (f32[2,1,16,4096]{3,2,1,0:T(8,128)S(1)}, f32[2,1,16,4096]{3,2,1,0:T(8,128)S(1)}, u32[]{:S(2)}, u32[]{:S(2)}) collective-permute-start(f32[2,1,16,4096]{3,2,1,0:T(8,128)S(1)} %get-tuple-element.14), channel_id=1, source_target_pairs={{1,0},{2,1},{3,2},{5,4},{6,5},{7,6},{9,8},{10,9},{11,10},{13,12},{... | collective-permute-start | bytes 1572872 | tf_op jit(solution)/shard_map/ppermute | solution.py:22
  92.1 3.4 %collective-permute-done.2 = f32[2,1,16,4096]{3,2,1,0:T(8,128)S(1)} collective-permute-done((f32[2,1,16,4096]{3,2,1,0:T(8,128)S(1)}, f32[2,1,16,4096]{3,2,1,0:T(8,128)S(1)}, u32[]{:S(2)}, u32[]{:S(2)}) %collective-permute-start.2) | collective-permute-done | bytes 524320 | tf_op jit(solution)/shard_map/ppermute | solution.py:20
  95.6 4.4 %collective-permute-done.3 = f32[2,1,16,4096]{3,2,1,0:T(8,128)S(1)} collective-permute-done((f32[2,1,16,4096]{3,2,1,0:T(8,128)S(1)}, f32[2,1,16,4096]{3,2,1,0:T(8,128)S(1)}, u32[]{:S(2)}, u32[]{:S(2)}) %collective-permute-start.3) | collective-permute-done | bytes 524320 | tf_op jit(solution)/shard_map/ppermute | solution.py:22
  102.8 1.0 fusion.9
  103.7 1.0 fusion.8
  105.9 1.0 convolution_subtract_fusion.2
  107.0 1.0 convolution_add_fusion.2
  108.1 1.0 pad_maximum_fusion.2
  (46 shorter events, 12.2 us)
Async XLA Ops:
  6.5 44.3 %all-gather.2.cloned.1.call-start = ((), (), s32[]{:S(2)}) async-start(), calls=%async_computation | async-start | bytes 1179648 | tf_op jit(solution)/shard_map/all_gather | solution.py:109
  59.1 11.3 %collective-permute-start = (f32[2,1,16,4096]{3,2,1,0:T(8,128)}, f32[2,1,16,4096]{3,2,1,0:T(8,128)}, u32[]{:S(2)}, u32[]{:S(2)}) collective-permute-start(f32[2,1,16,4096]{3,2,1,0:T(8,128)} %get-tuple-element.17), channel_id=1, source_target_pairs={{0,1},{1,2},{2,3},{4,5},{5,6},{6,7},{8,9},{9,10},{10,11},{12,13},{... | collective-permute-start | bytes 1572872 | tf_op jit(solution)/shard_map/ppermute | solution.py:20
  63.8 10.6 %collective-permute-start.1 = (f32[2,1,16,4096]{3,2,1,0:T(8,128)S(1)}, f32[2,1,16,4096]{3,2,1,0:T(8,128)}, u32[]{:S(2)}, u32[]{:S(2)}) collective-permute-start(f32[2,1,16,4096]{3,2,1,0:T(8,128)S(1)} %get-tuple-element.18), channel_id=1, source_target_pairs={{1,0},{2,1},{3,2},{5,4},{6,5},{7,6},{9,8},{10,9},{11,10},{13,12},{... | collective-permute-start | bytes 1572872 | tf_op jit(solution)/shard_map/ppermute | solution.py:22
  87.5 8.0 %collective-permute-start.2 = (f32[2,1,16,4096]{3,2,1,0:T(8,128)S(1)}, f32[2,1,16,4096]{3,2,1,0:T(8,128)S(1)}, u32[]{:S(2)}, u32[]{:S(2)}) collective-permute-start(f32[2,1,16,4096]{3,2,1,0:T(8,128)S(1)} %get-tuple-element.13), channel_id=1, source_target_pairs={{0,1},{1,2},{2,3},{4,5},{5,6},{6,7},{8,9},{9,10},{10,11},{12,13},{... | collective-permute-start | bytes 1572872 | tf_op jit(solution)/shard_map/ppermute | solution.py:20
  89.5 10.5 %collective-permute-start.3 = (f32[2,1,16,4096]{3,2,1,0:T(8,128)S(1)}, f32[2,1,16,4096]{3,2,1,0:T(8,128)S(1)}, u32[]{:S(2)}, u32[]{:S(2)}) collective-permute-start(f32[2,1,16,4096]{3,2,1,0:T(8,128)S(1)} %get-tuple-element.14), channel_id=1, source_target_pairs={{1,0},{2,1},{3,2},{5,4},{6,5},{7,6},{9,8},{10,9},{11,10},{13,12},{... | collective-permute-start | bytes 1572872 | tf_op jit(solution)/shard_map/ppermute | solution.py:22
Sparse Core Ops, SparseCore 0:
  9.5 41.2 all-gather.1
where the time goes:
time: 116 us
  waiting for transfers between devices  51.6 us (44%)
  local copies, waits for them, and re-layouts  15.7 us (14%)
  matrix products  14.8 us (13%)
  between operations  13.8 us (12%)
  starting transfers between devices  11.3 us (10%)
  other arithmetic  8.69 us (7%)
    all_gather x1, waiting for transfers between devices, body(): gathered = lax.all_gather(stored_planes, 'illum', axis=2, tiled=True)  39.1 us
    dot_general x8, matrix products, apply(): jnp.einsum('...nj,jc->...nc', win, kern, precision=lax.Precision.HIGHEST)  9.36 us
    ppermute x2, waiting for transfers between devices, extended(): lax.ppermute(head, axis, [((i + 1) % count, i) for i in range(ends)])  8.37 us
    ppermute x2, starting transfers between devices, extended(): lax.ppermute(tail, axis, [(i, (i + 1) % count) for i in range(ends)])  6.56 us
    dot_general x8, matrix products, apply(): jnp.einsum('ij,ajy->aiy', band, field, precision=lax.Precision.HIGHEST)  5.44 us
    ppermute x2, starting transfers between devices, extended(): lax.ppermute(head, axis, [((i + 1) % count, i) for i in range(ends)])  4.76 us
    sin x6, local copies, waits for them, and re-layouts, transmit(): sine = jnp.sin(screen)  4.53 us
    ppermute x2, waiting for transfers between devices, extended(): lax.ppermute(tail, axis, [(i, (i + 1) % count) for i in range(ends)])  3.44 us
  transfers between devices with their start and end apart: 5, of which 4 were waited for; matrix products, arithmetic and copies ran while one was open for 8% of the time, Pallas kernels for 0%

commit v1 on v0

--- a/solution.py
+++ b/solution.py
@@ -2,6 +2,7 @@
 import jax.numpy as jnp
 from jax import lax
 from jax.sharding import PartitionSpec as P
+from jax.lax import axis_index, axis_size, ppermute
 
 NY = 4096
 PLANES = 2
@@ -106,7 +107,15 @@
     total_rows = local_rows * lax.axis_size("tile")
     total_cols = NY
     first_row = lax.axis_index("tile") * local_rows
-    gathered = lax.all_gather(stored_planes, "illum", axis=2, tiled=True)
+    field_out, arr_next, f_now = (axis_size("illum"), axis_index("illum"), stored_planes.shape[2])
+    long_array, finding = (stored_planes, 1)
+    while finding < field_out:
+        tray = []
+        for src_i in range(field_out):
+            tray.append((src_i, (src_i - finding) % field_out))
+        long_array = jnp.concatenate([long_array, ppermute(long_array, "illum", perm=tray)], 2)
+        finding = 2 * finding
+    gathered = jnp.roll(long_array, arr_next * f_now, 2)
     screens = reorder(gathered, owner)
     extra = 0
     span = local_rows + 2 * extra

time: 116 us -> 99.2 us (0.86)
  between operations: 13.8 us -> 0.53 us
  waiting for transfers between devices: 51.6 us -> 40.5 us
  starting transfers between devices: 11.3 us -> 16.5 us
  other arithmetic: 8.69 us -> 10.4 us
    all_gather x1 -> x0, waiting for transfers between devices: 39.1 us -> none  [body(): gathered = lax.all_gather(stored_planes, 'illum', axis=2, tiled=True)]
    ppermute x0 -> x3, waiting for transfers between devices: none -> 28.7 us  [body(): ppermute(long_array, 'illum', perm=tray)]
    ppermute x0 -> x3, starting transfers between devices: none -> 6.17 us  [body(): ppermute(long_array, 'illum', perm=tray)]
    concatenate x0 -> x2, other arithmetic: none -> 1.86 us  [body(): jnp.concatenate([long_array, ppermute(long_array, 'illum', perm=tray)], 2)]
    slice x1, local copies, waits for them, and re-layouts: 1.27 us -> 0.08 us  [reorder(): gathered[p].reshape(count, blocks, width)[:, owner[p], :]]
    unnamed x14 -> x23, local copies, waits for them, and re-layouts: 2.72 us -> 3.75 us
  transfers between devices with their start and end apart: 5 -> 7, of which waited for: 4 -> 5; matrix products, arithmetic and copies ran while one was open for 8% -> 10% of each run, Pallas kernels for 0% -> 0%
where the time goes in v1:
time: 99.2 us; the launch traced here: 98.3 us
  waiting for transfers between devices  40.5 us (41%)
  starting transfers between devices  16.5 us (17%)
  local copies, waits for them, and re-layouts  15.5 us (16%)
  matrix products  14.8 us (15%)
  other arithmetic  10.4 us (10%)
    ppermute x3, waiting for transfers between devices, body(): ppermute(long_array, 'illum', perm=tray)  28.7 us
    dot_general x8, matrix products, apply(): jnp.einsum('...nj,jc->...nc', win, kern, precision=lax.Precision.HIGHEST)  9.37 us
    ppermute x2, waiting for transfers between devices, extended(): lax.ppermute(head, axis, [((i + 1) % count, i) for i in range(ends)])  8.37 us
    ppermute x3, starting transfers between devices, body(): ppermute(long_array, 'illum', perm=tray)  6.17 us
    ppermute x2, starting transfers between devices, extended(): lax.ppermute(tail, axis, [(i, (i + 1) % count) for i in range(ends)])  5.58 us
    dot_general x8, matrix products, apply(): jnp.einsum('ij,ajy->aiy', band, field, precision=lax.Precision.HIGHEST)  5.44 us
    ppermute x2, starting transfers between devices, extended(): lax.ppermute(head, axis, [((i + 1) % count, i) for i in range(ends)])  4.76 us
    sin x6, local copies, waits for them, and re-layouts, transmit(): sine = jnp.sin(screen)  4.53 us
  transfers between devices with their start and end apart: 7, of which 5 were waited for; matrix products, arithmetic and copies ran while one was open for 10% of the time, Pallas kernels for 0%

profile of v1, /device:TPU:1, one launch (start us, length us, event | category | flops | bytes accessed | tf_op | source)
XLA Modules:
  0.0 98.3 jit_solution(3632952811798959521)
XLA Ops:
  0.0 5.1 %collective-permute-start = (f32[2,32,512]{2,1,0:T(8,128)}, f32[2,32,512]{2,1,0:T(8,128)S(1)}, u32[]{:S(2)}, u32[]{:S(2)}) collective-permute-start(f32[2,32,512]{2,1,0:T(8,128)} %param.6), channel_id=1, source_target_pairs={{0,28},{4,0},{8,4},{12,8},{16,12},{20,16},{24,20},{28,24},{1,29},{... | collective-permute-start | bytes 393224 | tf_op jit(solution)/shard_map/ppermute | solution.py:116
  5.1 0.8 fusion.32
  5.9 1.3 %fusion.41 = (s32[1,1]{1,0:T(1,128)}, s32[1,1]{1,0:T(1,128)}) fusion(s32[1,2]{1,0:T(1,128)} %param.4), kind=kLoop, calls=%fused_computation.121 | loop fusion | bytes 16 | tf_op jit(solution)/shard_map/slice | solution.py:126
  7.8 0.9 pad_maximum_fusion.6
  8.7 1.0 %collective-permute-start.1 = (f32[2,32,1024]{2,1,0:T(8,128)S(1)}, f32[2,32,1024]{2,1,0:T(8,128)S(1)}, u32[]{:S(2)}, u32[]{:S(2)}) collective-permute-start(f32[2,32,1024]{2,1,0:T(8,128)S(1)} %pad_maximum_fusion.6), channel_id=1, source_target_pairs={{0,24},{4,28},{8,0},{12,4},{16,8},{20,12},{24,16},{28,20},{1,25},{... | collective-permute-start | bytes 786440 | tf_op jit(solution)/shard_map/ppermute | solution.py:116
  10.5 4.8 %collective-permute-done.1 = f32[2,32,1024]{2,1,0:T(8,128)S(1)} collective-permute-done((f32[2,32,1024]{2,1,0:T(8,128)S(1)}, f32[2,32,1024]{2,1,0:T(8,128)S(1)}, u32[]{:S(2)}, u32[]{:S(2)}) %collective-permute-start.1) | collective-permute-done | bytes 262176 | tf_op jit(solution)/shard_map/ppermute | solution.py:116
  15.2 0.9 pad_maximum_fusion.5
  16.9 0.9 constant_dynamic-update-slice_fusion.7
  18.1 23.9 %collective-permute-done.2 = f32[2,32,2048]{2,1,0:T(8,128)S(1)} collective-permute-done((f32[2,32,2048]{2,1,0:T(8,128)S(1)}, f32[2,32,2048]{2,1,0:T(8,128)S(1)}, u32[]{:S(2)}, u32[]{:S(2)}) %collective-permute-start.2) | collective-permute-done | bytes 524320 | tf_op jit(solution)/shard_map/ppermute | solution.py:116
  43.5 1.9 %sine_bitcast_fusion.1 = (f32[32,8,512]{2,0,1:T(8,128)S(1)}, f32[32,8,512]{2,0,1:T(8,128)S(1)}) fusion(f32[8,32,512]{2,1,0:T(8,128)S(1)} %gather_fusion), kind=kLoop, calls=%fused_computation.50 | loop fusion | bytes 1572864 | tf_op jit(solution)/shard_map/sin | solution.py:90
  46.2 2.2 %multiply_subtract_fusion.1 = (f32[1,1,32,4096]{3,2,1,0:T(8,128)S(1)}, f32[1,1,32,4096]{3,2,1,0:T(8,128)S(1)}) fusion(f32[1,1,32,4096]{3,2,1,0:T(8,128)S(1)} %sin.57, f32[1,1,32,4096]{3,2,1,0:T(8,128)S(1)} %cos.57, f32[4096]{0:T(1024)S(1)} %fusion.24, f32[32]{0:T(128)S(1)} %fusion.29, pred[32]{0:T(512)(128)(4,1)S(1)} %compare_and_fusion), kind=kLoop, calls=%fused_computation.63 | loop fusion | flops 1310720 | bytes 2113696 | tf_op jit(solution)/shard_map/sub | solution.py:91
  48.4 0.9 fusion.13
  49.3 3.7 %collective-permute-start.3 = (f32[2,1,16,4096]{3,2,1,0:T(8,128)}, f32[2,1,16,4096]{3,2,1,0:T(8,128)}, u32[]{:S(2)}, u32[]{:S(2)}) collective-permute-start(f32[2,1,16,4096]{3,2,1,0:T(8,128)} %get-tuple-element.17), channel_id=1, source_target_pairs={{0,1},{1,2},{2,3},{4,5},{5,6},{6,7},{8,9},{9,10},{10,11},{12,13},{... | collective-permute-start | bytes 1572872 | tf_op jit(solution)/shard_map/ppermute | solution.py:21
  52.9 2.1 %collective-permute-start.4 = (f32[2,1,16,4096]{3,2,1,0:T(8,128)S(1)}, f32[2,1,16,4096]{3,2,1,0:T(8,128)}, u32[]{:S(2)}, u32[]{:S(2)}) collective-permute-start(f32[2,1,16,4096]{3,2,1,0:T(8,128)S(1)} %get-tuple-element.18), channel_id=1, source_target_pairs={{1,0},{2,1},{3,2},{5,4},{6,5},{7,6},{9,8},{10,9},{11,10},{13,12},{... | collective-permute-start | bytes 1572872 | tf_op jit(solution)/shard_map/ppermute | solution.py:23
  56.8 1.9 %sine_bitcast_fusion = (f32[32,8,512]{2,0,1:T(8,128)S(1)}, f32[32,8,512]{2,0,1:T(8,128)S(1)}) fusion(f32[8,32,512]{2,1,0:T(8,128)S(1)} %gather_fusion.1), kind=kLoop, calls=%fused_computation.48 | loop fusion | bytes 1572864 | tf_op jit(solution)/shard_map/sin | solution.py:90
  59.6 4.0 %collective-permute-done.4 = f32[2,1,16,4096]{3,2,1,0:T(8,128)} collective-permute-done((f32[2,1,16,4096]{3,2,1,0:T(8,128)S(1)}, f32[2,1,16,4096]{3,2,1,0:T(8,128)}, u32[]{:S(2)}, u32[]{:S(2)}) %collective-permute-start.4) | collective-permute-done | bytes 524320 | tf_op jit(solution)/shard_map/ppermute | solution.py:23
  63.5 1.3 %pad_maximum_fusion = f32[2,1,64,4096]{3,2,1,0:T(8,128)S(1)} fusion(f32[2,1,16,4096]{3,2,1,0:T(8,128)} %collective-permute-done.4, f32[1,1,32,4096]{3,2,1,0:T(8,128)S(1)} %get-tuple-element.14, f32[1,1,32,4096]{3,2,1,0:T(8,128)S(1)} %get-tuple-element.13, f32[2,1,16,4096]{3,2,1,0:T(8,128)} %collective-permute-done.3), kind=kLoop, calls=%fused_computation.13 | loop fusion | flops 1572864 | bytes 4194304 | tf_op jit(solution)/shard_map/concatenate | solution.py:19
  68.7 1.0 fusion.11
  69.7 1.0 fusion.10
  70.7 1.8 %convolution_subtract_fusion.3 = f32[32,32,128]{2,1,0:T(8,128)} fusion(f32[32,32,128]{2,1,0:T(8,128)S(1)} %fusion.11, f32[1,32,32,32]{3,2,1,0:T(8,128)S(1)} %bitcast.154, f32[1,32,32,128]{3,2,1,0:T(8,128)S(1)} %bitcast.156, f32[160,128]{1,0:T(8,128)S(1)} %get-tuple-element.6), kind=kOutput, calls=%fused_computation.18 | convolution fusion | flops 251953152 | bytes 1785856 | tf_op jit(solution)/shard_map/...nj,jc->...nc/dot_general | solution.py:65
  72.5 1.1 %sub.181 = f32[1,1,32,4096]{3,2,1,0:T(8,128)S(1)} reshape(f32[32,32,128]{2,1,0:T(8,128)} %convolution_subtract_fusion.3) | data formatting | bytes 1048576 | tf_op jit(solution)/shard_map/sub | solution.py:69
  73.6 1.8 %convolution_add_fusion.3 = f32[32,32,128]{2,1,0:T(8,128)} fusion(f32[32,32,128]{2,1,0:T(8,128)S(1)} %fusion.10, f32[1,32,32,32]{3,2,1,0:T(8,128)S(1)} %bitcast.155, f32[1,32,32,128]{3,2,1,0:T(8,128)S(1)} %bitcast.157, f32[160,128]{1,0:T(8,128)S(1)} %get-tuple-element.5), kind=kOutput, calls=%fused_computation.17 | convolution fusion | flops 251953152 | bytes 1785856 | tf_op jit(solution)/shard_map/...nj,jc->...nc/dot_general | solution.py:65
  75.4 1.1 %add.196 = f32[1,1,32,4096]{3,2,1,0:T(8,128)S(1)} reshape(f32[32,32,128]{2,1,0:T(8,128)} %convolution_add_fusion.3) | data formatting | bytes 1048576 | tf_op jit(solution)/shard_map/add | solution.py:70
  76.7 1.9 %collective-permute-start.5 = (f32[2,1,16,4096]{3,2,1,0:T(8,128)S(1)}, f32[2,1,16,4096]{3,2,1,0:T(8,128)S(1)}, u32[]{:S(2)}, u32[]{:S(2)}) collective-permute-start(f32[2,1,16,4096]{3,2,1,0:T(8,128)S(1)} %get-tuple-element.15), channel_id=1, source_target_pairs={{0,1},{1,2},{2,3},{4,5},{5,6},{6,7},{8,9},{9,10},{10,11},{12,13},{... | collective-permute-start | bytes 1572872 | tf_op jit(solution)/shard_map/ppermute | solution.py:21
  78.6 2.7 %collective-permute-start.6 = (f32[2,1,16,4096]{3,2,1,0:T(8,128)S(1)}, f32[2,1,16,4096]{3,2,1,0:T(8,128)S(1)}, u32[]{:S(2)}, u32[]{:S(2)}) collective-permute-start(f32[2,1,16,4096]{3,2,1,0:T(8,128)S(1)} %get-tuple-element.16), channel_id=1, source_target_pairs={{1,0},{2,1},{3,2},{5,4},{6,5},{7,6},{9,8},{10,9},{11,10},{13,12},{... | collective-permute-start | bytes 1572872 | tf_op jit(solution)/shard_map/ppermute | solution.py:23
  81.3 3.4 %collective-permute-done.5 = f32[2,1,16,4096]{3,2,1,0:T(8,128)S(1)} collective-permute-done((f32[2,1,16,4096]{3,2,1,0:T(8,128)S(1)}, f32[2,1,16,4096]{3,2,1,0:T(8,128)S(1)}, u32[]{:S(2)}, u32[]{:S(2)}) %collective-permute-start.5) | collective-permute-done | bytes 524320 | tf_op jit(solution)/shard_map/ppermute | solution.py:21
  84.7 4.4 %collective-permute-done.6 = f32[2,1,16,4096]{3,2,1,0:T(8,128)S(1)} collective-permute-done((f32[2,1,16,4096]{3,2,1,0:T(8,128)S(1)}, f32[2,1,16,4096]{3,2,1,0:T(8,128)S(1)}, u32[]{:S(2)}, u32[]{:S(2)}) %collective-permute-start.6) | collective-permute-done | bytes 524320 | tf_op jit(solution)/shard_map/ppermute | solution.py:23
  91.9 1.0 fusion.9
  92.9 1.0 fusion.8
  95.1 1.0 convolution_subtract_fusion.2
  96.2 1.0 convolution_add_fusion.2
  97.3 1.0 %pad_maximum_fusion.2 = f32[2,1,32,4096]{3,2,1,0:T(8,128)} fusion(f32[1,1,32,4096]{3,2,1,0:T(8,128)S(1)} %add.202, f32[1,1,32,4096]{3,2,1,0:T(8,128)S(1)} %sub.187), kind=kLoop, calls=%fused_computation.31 | loop fusion | flops 262144 | bytes 2097152 | tf_op jit(solution)/shard_map/stack | solution.py:137
  (61 shorter events, 15.2 us)
Async XLA Ops:
  0.0 42.1 %copy-start = (f32[2,32,512]{2,1,0:T(8,128)S(1)}, f32[2,32,512]{2,1,0:T(8,128)}, u32[]{:S(2)}) copy-start(f32[2,32,512]{2,1,0:T(8,128)} %param.6) | copy-start | bytes 393220
  0.0 7.8 %collective-permute-start = (f32[2,32,512]{2,1,0:T(8,128)}, f32[2,32,512]{2,1,0:T(8,128)S(1)}, u32[]{:S(2)}, u32[]{:S(2)}) collective-permute-start(f32[2,32,512]{2,1,0:T(8,128)} %param.6), channel_id=1, source_target_pairs={{0,28},{4,0},{8,4},{12,8},{16,12},{20,16},{24,20},{28,24},{1,29},{... | collective-permute-start | bytes 393224 | tf_op jit(solution)/shard_map/ppermute | solution.py:116
  8.7 6.5 %collective-permute-start.1 = (f32[2,32,1024]{2,1,0:T(8,128)S(1)}, f32[2,32,1024]{2,1,0:T(8,128)S(1)}, u32[]{:S(2)}, u32[]{:S(2)}) collective-permute-start(f32[2,32,1024]{2,1,0:T(8,128)S(1)} %pad_maximum_fusion.6), channel_id=1, source_target_pairs={{0,24},{4,28},{8,0},{12,4},{16,8},{20,12},{24,16},{28,20},{1,25},{... | collective-permute-start | bytes 786440 | tf_op jit(solution)/shard_map/ppermute | solution.py:116
  16.2 25.9 %collective-permute-start.2 = (f32[2,32,2048]{2,1,0:T(8,128)S(1)}, f32[2,32,2048]{2,1,0:T(8,128)S(1)}, u32[]{:S(2)}, u32[]{:S(2)}) collective-permute-start(f32[2,32,2048]{2,1,0:T(8,128)S(1)} %pad_maximum_fusion.5), channel_id=1, source_target_pairs={{0,16},{4,20},{8,24},{12,28},{16,0},{20,4},{24,8},{28,12},{1,17},{... | collective-permute-start | bytes 1572872 | tf_op jit(solution)/shard_map/ppermute | solution.py:116
  49.3 10.3 %collective-permute-start.3 = (f32[2,1,16,4096]{3,2,1,0:T(8,128)}, f32[2,1,16,4096]{3,2,1,0:T(8,128)}, u32[]{:S(2)}, u32[]{:S(2)}) collective-permute-start(f32[2,1,16,4096]{3,2,1,0:T(8,128)} %get-tuple-element.17), channel_id=1, source_target_pairs={{0,1},{1,2},{2,3},{4,5},{5,6},{6,7},{8,9},{9,10},{10,11},{12,13},{... | collective-permute-start | bytes 1572872 | tf_op jit(solution)/shard_map/ppermute | solution.py:21
  52.9 10.6 %collective-permute-start.4 = (f32[2,1,16,4096]{3,2,1,0:T(8,128)S(1)}, f32[2,1,16,4096]{3,2,1,0:T(8,128)}, u32[]{:S(2)}, u32[]{:S(2)}) collective-permute-start(f32[2,1,16,4096]{3,2,1,0:T(8,128)S(1)} %get-tuple-element.18), channel_id=1, source_target_pairs={{1,0},{2,1},{3,2},{5,4},{6,5},{7,6},{9,8},{10,9},{11,10},{13,12},{... | collective-permute-start | bytes 1572872 | tf_op jit(solution)/shard_map/ppermute | solution.py:23
  76.7 8.0 %collective-permute-start.5 = (f32[2,1,16,4096]{3,2,1,0:T(8,128)S(1)}, f32[2,1,16,4096]{3,2,1,0:T(8,128)S(1)}, u32[]{:S(2)}, u32[]{:S(2)}) collective-permute-start(f32[2,1,16,4096]{3,2,1,0:T(8,128)S(1)} %get-tuple-element.15), channel_id=1, source_target_pairs={{0,1},{1,2},{2,3},{4,5},{5,6},{6,7},{8,9},{9,10},{10,11},{12,13},{... | collective-permute-start | bytes 1572872 | tf_op jit(solution)/shard_map/ppermute | solution.py:21
  78.6 10.5 %collective-permute-start.6 = (f32[2,1,16,4096]{3,2,1,0:T(8,128)S(1)}, f32[2,1,16,4096]{3,2,1,0:T(8,128)S(1)}, u32[]{:S(2)}, u32[]{:S(2)}) collective-permute-start(f32[2,1,16,4096]{3,2,1,0:T(8,128)S(1)} %get-tuple-element.16), channel_id=1, source_target_pairs={{1,0},{2,1},{3,2},{5,4},{6,5},{7,6},{9,8},{10,9},{11,10},{13,12},{... | collective-permute-start | bytes 1572872 | tf_op jit(solution)/shard_map/ppermute | solution.py:23
